TPU v7x, 512 devices: a whole 4x4x16 slice. The times are simulated.
512 devices in a mesh: dp: 32 (over y_hi, z), tensor: 16 (over x, y_lo, core).
Axes of the slice: x: 4, y: 4 (y_hi: 2, y_lo: 2; y = y_hi * 2 + y_lo), z: 16, core: 2. Of those that a mesh axis runs over, the one named last changes fastest.
Arguments:
- residual: bfloat16 [65536, 2048], P(('dp', 'tensor')), may hold values from -0.59765625 to 0.59765625
- queries: bfloat16 [65536, 2048], P(('dp', 'tensor')), may hold values from -27 to 27
- new_keys: bfloat16 [65536, 2048], P(('dp', 'tensor')), may hold values from -27 to 27
- new_values: bfloat16 [65536, 2048], P(('dp', 'tensor')), may hold values from -6 to 6
- lengths: int32 [32, 2], P('dp'), may hold values from 1 to 1536, 2048 in all within a row
- page_order: int32 [32, 17], P('dp'), may hold values from 0 to 16, each once within a row
- wo_shard: float32 [2048, 2048], P('tensor', 'dp'), may hold values from -0.125 to 0.125
- norm_gain: float32 [2048], replicated, may hold values from 0.1 to 1.9
- gate_shard: float32 [16, 2048, 256], P('tensor', 'dp'), may hold values from -0.125 to 0.125
- up_shard: float32 [16, 2048, 256], P('tensor', 'dp'), may hold values from -0.125 to 0.125
- down_shard: float32 [16, 256, 2048], P('tensor', None, 'dp'), may hold values from -0.1875 to 0.1875
- routes: int32 [65536, 8], P(('dp', 'tensor')), may hold values from 0 to 63, as said below
- route_weights: float32 [65536, 8], P(('dp', 'tensor')), may hold values from 0.05 to 0.3
Outputs:
- hidden_mid: bfloat16 [65536, 2048], P(('dp', 'tensor'))
- expert_sum: bfloat16 [65536, 2048], P(('dp', 'tensor'))
- key_pages: bfloat16 [544, 128, 2048], P('dp', None, 'tensor')
- value_pages: bfloat16 [544, 128, 2048], P('dp', None, 'tensor')
Inputs may be any that keep to these rules, and one draw needn't show every extreme that they name: `routes`: each row names 8 different experts. Within each aligned block of 128 rows (the rows of one device), each expert below 4 is named by 1 to 16 rows; one of them, the same in all blocks of a draw, by exactly 16 rows in every block, the others by at most 8 rows.
All inputs are finite; a program needn't handle non-finite values.
Results may differ from a plain program's by a relative error of at most 0.015.
Values may be sent and summed in bfloat16 or wider, within the bound.
No kernel may reach another device: no remote copies, remote signals or barrier semaphores. Data moves between devices by JAX's collectives and lax.ppermute only.
A program may use at most 64 MiB of HBM per device.

v0:
```python
import math
import jax
import jax.numpy as jnp
from jax import lax
from jax.sharding import Mesh, PartitionSpec as P

D = 2048
HEADS = 16
HD = 128
SPLIT = 4
PAGE = 128
MOST = 16


def page_layout(lens_row, order_row, group_rows, pool_size):
    index_rows = jnp.arange(group_rows, dtype=jnp.int32)
    prompt_ends = jnp.cumsum(lens_row)
    segment = jnp.sum((index_rows[:, None] >= prompt_ends[None, :]).astype(jnp.int32), axis=1)
    prompt_starts = prompt_ends - lens_row
    owner_mask = (
        segment[:, None] == jnp.arange(lens_row.shape[0], dtype=jnp.int32)[None, :]
    ).astype(jnp.int32)
    begins = jnp.sum(owner_mask * prompt_starts[None, :], axis=1)
    page_count = (lens_row + PAGE - 1) // PAGE
    first_page = jnp.cumsum(page_count) - page_count
    page_first = jnp.sum(owner_mask * first_page[None, :], axis=1)
    position = index_rows - begins
    logical = page_first + position // PAGE
    matched = (logical[:, None] == jnp.arange(pool_size, dtype=jnp.int32)[None, :]).astype(
        jnp.int32
    )
    physical = jnp.sum(matched * order_row[None, :], axis=1)
    return (segment, physical * PAGE + position % PAGE)


def attend_group(q_heads, k_heads, v_heads, segment, heads_here):
    group_rows = q_heads.shape[0]
    block_rows = min(512, group_rows)
    count_blocks = group_rows // block_rows
    q_blocks = q_heads.reshape(count_blocks, block_rows, heads_here, HD)
    seg_blocks = segment.reshape(count_blocks, block_rows)
    k_split = k_heads.reshape(group_rows, heads_here, HD)
    v_split = v_heads.reshape(group_rows, heads_here, HD)

    def one_block(block_pair):
        q_block, seg_block = block_pair
        scores = jnp.einsum(
            "qhd,khd->hqk", q_block, k_split, preferred_element_type=jnp.float32
        ) / math.sqrt(HD)
        same_prompt = seg_block[:, None] == segment[None, :]
        scores = jnp.where(same_prompt[None, :, :], scores, -jnp.inf)
        row_max = jnp.max(scores, axis=2, keepdims=True)
        weights = jnp.exp(scores - row_max)
        totals = jnp.sum(weights, axis=2)
        output = jnp.einsum(
            "hqk,khd->qhd",
            weights.astype(jnp.bfloat16),
            v_split,
            preferred_element_type=jnp.float32,
        )
        output = output / jnp.transpose(totals)[:, :, None]
        return output.astype(jnp.bfloat16).reshape(block_rows, heads_here * HD)

    return lax.map(one_block, (q_blocks, seg_blocks)).reshape(group_rows, heads_here * HD)


def body(
    residual,
    queries,
    new_keys,
    new_values,
    lengths,
    page_order,
    wo_shard,
    norm_gain,
    gate_shard,
    up_shard,
    down_shard,
    routes,
    route_weights,
):
    tensor_count = lax.axis_size("tensor")
    heads_here = HEADS // tensor_count
    q_heads, k_heads, v_heads = (
        lax.all_to_all(queries, "tensor", split_axis=1, concat_axis=0, tiled=True),
        lax.all_to_all(new_keys, "tensor", split_axis=1, concat_axis=0, tiled=True),
        lax.all_to_all(new_values, "tensor", split_axis=1, concat_axis=0, tiled=True),
    )
    group_rows = q_heads.shape[0]
    pool_size = page_order.shape[1]
    segment, slot_index = page_layout(lengths[0], page_order[0], group_rows, pool_size)
    head_width = k_heads.shape[1]
    key_pages = (
        jnp.zeros((pool_size * PAGE, head_width), jnp.bfloat16)
        .at[slot_index]
        .set(k_heads)
        .reshape(pool_size, PAGE, head_width)
    )
    value_pages = (
        jnp.zeros((pool_size * PAGE, head_width), jnp.bfloat16)
        .at[slot_index]
        .set(v_heads)
        .reshape(pool_size, PAGE, head_width)
    )
    pieces = [
        wo_shard.astype(jnp.bfloat16).T,
        gate_shard[0].astype(jnp.bfloat16),
        up_shard[0].astype(jnp.bfloat16),
        down_shard[0].astype(jnp.bfloat16),
    ]
    packed = jnp.concatenate([p.reshape(-1) for p in pieces]).reshape(-1, 128)
    gathered = lax.all_gather(lax.all_gather(packed, "dh"), "dz")
    gathered, q_heads, k_heads, v_heads, key_pages, value_pages = lax.optimization_barrier(
        (gathered, q_heads, k_heads, v_heads, key_pages, value_pages)
    )
    wo_piece_rows = pieces[0].size // 128
    wo_cols = jnp.swapaxes(gathered[:, :, :wo_piece_rows], 0, 1).reshape(-1, pieces[0].shape[1])
    wo_full = lax.all_gather(wo_cols, "tensor", axis=1, tiled=True)
    experts = jnp.swapaxes(gathered[:, :, wo_piece_rows:], 0, 1)
    experts = experts.reshape(experts.shape[0] * experts.shape[1], -1)
    weights_full, at = ([], 0)
    for p in pieces[1:]:
        weights_full.append(experts[:, at : at + p.size].reshape((-1,) + p.shape))
        at += p.size
    gate_full = weights_full[0].reshape(1, -1, gate_shard.shape[2])
    up_full = weights_full[1].reshape(1, -1, up_shard.shape[2])
    down_full = weights_full[2].transpose(1, 0, 2).reshape(1, down_shard.shape[1], -1)
    attended = attend_group(q_heads, k_heads, v_heads, segment, heads_here)
    token_rows = lax.all_to_all(attended, "tensor", split_axis=0, concat_axis=1, tiled=True)
    projected = jnp.einsum("tr,cr->tc", token_rows, wo_full, preferred_element_type=jnp.float32)
    hidden_mid = (residual.astype(jnp.float32) + projected).astype(jnp.bfloat16)
    mid_float = hidden_mid.astype(jnp.float32)
    normed = (
        mid_float
        * lax.rsqrt(jnp.mean(mid_float * mid_float, axis=1, keepdims=True) + 1e-06)
        * norm_gain
    ).astype(jnp.bfloat16)
    flight = tensor_count // SPLIT
    flight_ids = jnp.arange(flight, dtype=jnp.int32)
    named_here = routes[:, :, None] == flight_ids[None, None, :]
    routed = jnp.any(named_here, axis=1)
    weight_sum = jnp.sum(jnp.where(named_here, route_weights[:, :, None], 0.0), axis=1)
    ranked = jnp.cumsum(routed.astype(jnp.int32), axis=0) - 1
    picked = (ranked[:, :, None] == jnp.arange(MOST, dtype=jnp.int32)[None, None, :]) & routed[
        :, :, None
    ]
    outgoing = jnp.einsum(
        "tem,td->emd", picked.astype(jnp.bfloat16), normed, preferred_element_type=jnp.float32
    ).astype(jnp.bfloat16)
    outgoing = jnp.repeat(outgoing, SPLIT, axis=0)
    arrived = lax.all_to_all(outgoing, "tensor", split_axis=0, concat_axis=0, tiled=True)
    gate_val = jnp.einsum("smd,dp->smp", arrived, gate_full[0], preferred_element_type=jnp.float32)
    up_val = jnp.einsum("smd,dp->smp", arrived, up_full[0], preferred_element_type=jnp.float32)
    inner_act = (jax.nn.silu(gate_val) * up_val).astype(jnp.bfloat16)
    result = jnp.einsum(
        "smp,pd->smd", inner_act, down_full[0], preferred_element_type=jnp.float32
    ).astype(jnp.bfloat16)
    returned = lax.all_to_all(result, "tensor", split_axis=0, concat_axis=0, tiled=True)
    summed = jnp.sum(returned.reshape(flight, SPLIT, MOST, D).astype(jnp.float32), axis=1)
    mixing = picked.astype(jnp.float32) * weight_sum[:, :, None]
    expert_sum = jnp.einsum("tem,emd->td", mixing, summed, precision=lax.Precision.HIGHEST).astype(
        jnp.bfloat16
    )
    return (hidden_mid, expert_sum, key_pages, value_pages)


def solution(mesh):
    dp_count = mesh.shape["dp"]
    dz_count = 16 if dp_count % 16 == 0 else dp_count
    split_mesh = Mesh(
        mesh.devices.reshape(dp_count // dz_count, dz_count, mesh.shape["tensor"]),
        ("dh", "dz", "tensor"),
    )
    return jax.shard_map(
        body,
        mesh=split_mesh,
        in_specs=(
            P(("dh", "dz", "tensor"), None),
            P(("dh", "dz", "tensor"), None),
            P(("dh", "dz", "tensor"), None),
            P(("dh", "dz", "tensor"), None),
            P(("dh", "dz"), None),
            P(("dh", "dz"), None),
            P("tensor", ("dh", "dz")),
            P(),
            P("tensor", ("dh", "dz"), None),
            P("tensor", ("dh", "dz"), None),
            P("tensor", None, ("dh", "dz")),
            P(("dh", "dz", "tensor"), None),
            P(("dh", "dz", "tensor"), None),
        ),
        out_specs=(
            P(("dh", "dz", "tensor"), None),
            P(("dh", "dz", "tensor"), None),
            P(("dh", "dz"), None, "tensor"),
            P(("dh", "dz"), None, "tensor"),
        ),
        check_vma=False,
    )
```

profile of v0, /device:TPU:224, one launch (start us, length us, event | category | flops | bytes accessed | tf_op | source)
XLA Modules:
  0.0 236.6 jit_solution(14341236253968236352)
XLA Ops:
  7.2 0.8 convert_bitcast_fusion.2
  8.1 0.8 convert_bitcast_fusion.1
  9.0 0.8 convert_bitcast_fusion
  9.8 0.8 convert_element_type.85
  10.7 0.1 copy.64
  10.8 0.1 convert_element_type.86
  10.9 7.2 %all_gather.12 = bf16[2,448,128]{2,1,0:T(8,128)(2,1)} all-gather(bf16[1,448,128]{2,1,0:T(8,128)(2,1)S(1)} %maximum_bitcast_fusion), channel_id=1, replica_groups=mesh['dh'=2,'dz'=16,'tensor'=16] {'dh'}, dimensions={0}, use_global_device_ids=true | all-gather | bytes 344064 | tf_op jit(solution)/shard_map/all_gather | solution.py:112
  18.1 0.9 copy_bitcast_fusion.2
  19.1 5.4 %all-to-all-start.1 = ((bf16[128,16,128]{2,0,1:T(8,128)(2,1)}), bf16[128,16,128]{2,0,1:T(8,128)(2,1)S(1)}, u32[]{:S(2)}, u32[]{:S(2)}) async-start(bf16[128,16,128]{2,0,1:T(8,128)(2,1)} %copy_bitcast_fusion.2), calls=%async_computation.1 | async-start | bytes 1048576 | tf_op jit(solution)/shard_map/all_to_all | solution.py:86
  24.5 0.8 reduce-window.6
  25.3 0.7 and_select_fusion.1
  26.0 0.2 reduce-window_1_clone.1
  26.2 0.1 fusion.49
  26.3 0.1 select_reduce_fusion.2
  26.4 2.0 copy_bitcast_fusion.1
  28.4 7.0 %all-to-all-done.1 = bf16[128,16,128]{2,0,1:T(8,128)(2,1)S(1)} async-done(((bf16[128,16,128]{2,0,1:T(8,128)(2,1)}), bf16[128,16,128]{2,0,1:T(8,128)(2,1)S(1)}, u32[]{:S(2)}, u32[]{:S(2)}) %all-to-all-start.1) | async-done | bytes 524320 | tf_op jit(solution)/shard_map/all_to_all | solution.py:86
  35.3 3.6 %all-to-all-start.2 = ((bf16[128,16,128]{2,0,1:T(8,128)(2,1)}), bf16[128,16,128]{2,0,1:T(8,128)(2,1)S(1)}, u32[]{:S(2)}, u32[]{:S(2)}) async-start(bf16[128,16,128]{2,0,1:T(8,128)(2,1)} %copy_bitcast_fusion.1), calls=%async_computation.2 | async-start | bytes 1048576 | tf_op jit(solution)/shard_map/all_to_all | solution.py:87
  38.9 0.1 select_reduce_fusion
  39.0 0.9 copy_bitcast_fusion.3
  40.0 9.7 %all-to-all-done.2 = bf16[128,16,128]{2,0,1:T(8,128)(2,1)S(1)} async-done(((bf16[128,16,128]{2,0,1:T(8,128)(2,1)}), bf16[128,16,128]{2,0,1:T(8,128)(2,1)S(1)}, u32[]{:S(2)}, u32[]{:S(2)}) %all-to-all-start.2) | async-done | bytes 524320 | tf_op jit(solution)/shard_map/all_to_all | solution.py:87
  49.7 3.6 %all-to-all-start = ((bf16[128,16,128]{2,0,1:T(8,128)(2,1)}), bf16[128,16,128]{2,0,1:T(8,128)(2,1)S(1)}, u32[]{:S(2)}, u32[]{:S(2)}) async-start(bf16[128,16,128]{2,0,1:T(8,128)(2,1)} %copy_bitcast_fusion.3), calls=%async_computation | async-start | bytes 1048576 | tf_op jit(solution)/shard_map/all_to_all | solution.py:85
  53.4 6.5 %scatter_custom_fusion.1 = bf16[2176,128]{1,0:T(8,128)(2,1)} fusion(s32[2048]{0:T(1024)S(1)} %bitcast.161, bf16[2048,128]{1,0:T(8,128)(2,1)S(1)} %bitcast.140, bf16[]{:T(256)} %constant.81.clone.1), kind=kCustom, calls=%fused_computation.42 | custom fusion | bytes 557058 | tf_op jit(solution)/shard_map/scatter | solution.py:102
  59.9 6.5 %scatter_custom_fusion = bf16[2176,128]{1,0:T(8,128)(2,1)} fusion(s32[2048]{0:T(1024)S(1)} %bitcast.162, bf16[2048,128]{1,0:T(8,128)(2,1)S(1)} %bitcast.153, bf16[]{:T(256)} %constant.81.clone.1), kind=kCustom, calls=%fused_computation.44 | custom fusion | bytes 557058 | tf_op jit(solution)/shard_map/scatter | solution.py:96
  66.5 27.6 %all-gather.6.cloned.1.call-done = bf16[32,448,128]{2,1,0:T(8,128)(2,1)} async-done(((bf16[2,448,128]{2,1,0:T(8,128)(2,1)}), bf16[32,448,128]{2,1,0:T(8,128)(2,1)}) %all-gather.6.cloned.1.call-update) | async-done | bytes 3670032 | tf_op jit(solution)/shard_map/all_gather | solution.py:112
  94.0 1.1 slice_bitcast_fusion.1
  95.1 0.8 copy.70
  96.0 0.1 copy.71
  96.1 0.2 reduce_window_sum.20
  96.3 12.2 %while.10 = (s32[]{:T(128)}, bf16[4,512,128]{2,1,0:T(8,128)(2,1)}, s32[4,512]{1,0:T(4,128)S(1)}, s32[2048]{0:T(1024)S(1)}, bf16[4,512,1,128]{3,1,2,0:T(8,128)(2,...) while((s32[]{:T(128)}, bf16[4,512,128]{2,1,0:T(8,128)(2,1)}, ...), condition=%wide.region_11.12_spmd, body=%wide.region_8.11_spmd.sunk | while | flops 545389568 | bytes 13918313 | solution.py:64
  96.3 0.9 fusion.86
  97.2 0.7 fusion.87
  97.9 1.5 fusion.88
  99.4 0.9 fusion.86
  100.3 0.7 fusion.87
  101.0 1.5 fusion.88
  102.4 0.9 fusion.86
  103.3 0.7 fusion.87
  104.0 1.5 fusion.88
  105.5 0.9 fusion.86
  106.4 0.7 fusion.87
  107.1 1.5 fusion.88
  108.5 5.3 %all-to-all-start.3 = ((bf16[16,128,128]{2,1,0:T(8,128)(2,1)}), bf16[16,128,128]{2,1,0:T(8,128)(2,1)S(1)}, u32[]{:S(2)}, u32[]{:S(2)}) async-start(bf16[16,128,128]{2,1,0:T(8,128)(2,1)} %bitcast.35), calls=%async_computation.3 | async-start | bytes 1048576 | tf_op jit(solution)/shard_map/all_to_all | solution.py:129
  113.9 2.3 slice_bitcast_fusion
  116.2 0.3 copy.73
  116.6 3.8 %copy.88 = bf16[4,8,384,128]{3,1,2,0:T(8,128)(2,1)} copy(bf16[4,8,384,128]{3,2,1,0:T(8,128)(2,1)S(1)} %bitcast.143) | data formatting | bytes 6291456
  120.4 7.0 %all-to-all-done.3 = bf16[16,128,128]{2,1,0:T(8,128)(2,1)S(1)} async-done(((bf16[16,128,128]{2,1,0:T(8,128)(2,1)}), bf16[16,128,128]{2,1,0:T(8,128)(2,1)S(1)}, u32[]{:S(2)}, u32[]{:S(2)}) %all-to-all-start.3) | async-done | bytes 524320 | tf_op jit(solution)/shard_map/all_to_all | solution.py:129
  127.4 0.3 copy.69
  127.6 43.4 %all-gather.4.cloned.1.call-done = bf16[2048,2048]{1,0:T(8,128)(2,1)} async-done(((bf16[2048,128]{1,0:T(8,128)(2,1)}), bf16[2048,2048]{1,0:T(8,128)(2,1)}) %all-gather.4.cloned.1.call-update) | async-done | bytes 8388624 | tf_op jit(solution)/shard_map/all_gather | solution.py:118
  171.1 6.4 %fusion.28 = (f32[128]{0:T(128)S(1)}, bf16[128,2048]{1,0:T(8,128)(2,1)S(1)}) fusion(bf16[128,2048]{0,1:T(8,128)(2,1)S(1)} %bitcast.147, bf16[2048,2048]{1,0:T(8,128)(2,1)} %all-gather.4.cloned.1.call-done, bf16[128,2048]{1,0:T(8,128)(2,1)S(1)} %copy-done.1), kind=kOutput, calls=%fused_computation.32 | convolution fusion | flops 1075314560 | bytes 9961984 | tf_op jit(solution)/shard_map/tr,cr->tc/dot_general | solution.py:130
  177.5 0.3 convolution_convert_fusion.1
  177.8 1.2 broadcast_in_dim.27
  179.0 6.1 %all-to-all-start.4 = ((bf16[16,16,2048]{2,1,0:T(8,128)(2,1)}), bf16[16,16,2048]{2,1,0:T(8,128)(2,1)}, u32[]{:S(2)}, u32[]{:S(2)}) async-start(bf16[16,16,2048]{2,1,0:T(8,128)(2,1)} %bitcast.41), calls=%async_computation.4 | async-start | bytes 2097152 | tf_op jit(solution)/shard_map/all_to_all | solution.py:151
  185.0 3.0 %fusion.66 = (bf16[32,16384]{1,0:T(8,128)(2,1)S(1)}, bf16[32,16384]{1,0:T(8,128)(2,1)}, bf16[32,16384]{1,0:T(8,128)(2,1)S(1)}) fusion(bf16[32,49152]{1,0:T(8,128)(2,1)} %bitcast.142), kind=kLoop, calls=%fused_computation.103 | loop fusion | bytes 6291456 | tf_op jit(solution)/shard_map/slice | solution.py:123
  188.1 1.3 reshape.276
  189.4 1.3 reshape.277
  190.7 3.0 %reshape.256 = bf16[32,256,64]{2,1,0:T(8,128)(2,1)S(1)} reshape(bf16[32,16384]{1,0:T(8,128)(2,1)} %get-tuple-element.101) | data formatting | bytes 2097152 | tf_op jit(solution)/shard_map/reshape | solution.py:123
  193.8 1.6 copy.74
  195.4 6.2 %all-to-all-done.4 = bf16[16,16,2048]{2,1,0:T(8,128)(2,1)} async-done(((bf16[16,16,2048]{2,1,0:T(8,128)(2,1)}), bf16[16,16,2048]{2,1,0:T(8,128)(2,1)}, u32[]{:S(2)}, u32[]{:S(2)}) %all-to-all-start.4) | async-done | bytes 1048608 | tf_op jit(solution)/shard_map/all_to_all | solution.py:151
  201.5 2.0 fusion.67
  203.5 4.2 %convolution_convert_fusion = bf16[16,16,2048]{2,1,0:T(8,128)(2,1)} fusion(bf16[256,2048,1]{0,1,2:T(8,128)(2,1)} %bitcast.150, bf16[16,16,2048]{2,1,0:T(8,128)(2,1)} %all-to-all-done.4, bf16[2048,256,1]{1,0,2:T(8,128)(2,1)} %reshape.277, f32[16,16,256]{2,1,0:T(8,128)S(1)} %fusion.67), kind=kOutput, calls=%fused_computation.21 | convolution fusion | flops 537788416 | bytes 4456448 | tf_op jit(solution)/shard_map/smp,pd->smd/dot_general | solution.py:155
  207.7 3.7 %all-to-all-start.5 = ((bf16[16,16,2048]{2,1,0:T(8,128)(2,1)}), bf16[16,16,2048]{2,1,0:T(8,128)(2,1)S(1)}, u32[]{:S(2)}, u32[]{:S(2)}) async-start(bf16[16,16,2048]{2,1,0:T(8,128)(2,1)} %convolution_convert_fusion), calls=%async_computation.5 | async-start | bytes 2097152 | tf_op jit(solution)/shard_map/all_to_all | solution.py:158
  211.4 16.4 %all-to-all-done.5 = bf16[16,16,2048]{2,1,0:T(8,128)(2,1)S(1)} async-done(((bf16[16,16,2048]{2,1,0:T(8,128)(2,1)}), bf16[16,16,2048]{2,1,0:T(8,128)(2,1)S(1)}, u32[]{:S(2)}, u32[]{:S(2)}) %all-to-all-start.5) | async-done | bytes 1048608 | tf_op jit(solution)/shard_map/all_to_all | solution.py:158
  227.8 0.2 convert_reduce_fusion
  227.9 1.8 fusion.26
  (40 shorter events, 0.5 us)
Async XLA Ops:
  7.2 11.0 %copy-start = (bf16[128,2048]{1,0:T(8,128)(2,1)S(1)}, bf16[128,2048]{1,0:T(8,128)(2,1)}, u32[]{:S(2)}) copy-start(bf16[128,2048]{1,0:T(8,128)(2,1)} %param.17) | copy-start | bytes 1572868
  7.2 31.7 %copy-start.6 = (s32[1,17]{1,0:T(1,128)S(1)}, s32[1,17]{1,0:T(1,128)}, u32[]{:S(2)}) copy-start(s32[1,17]{1,0:T(1,128)} %param.20) | copy-start | bytes 208
  7.2 31.8 %copy-start.3 = (bf16[128,2048]{1,0:T(8,128)(2,1)S(1)}, bf16[128,2048]{1,0:T(8,128)(2,1)}, u32[]{:S(2)}) copy-start(bf16[128,2048]{1,0:T(8,128)(2,1)} %param.16) | copy-start | bytes 1572868
  7.2 86.8 %all-gather.6.cloned.1.call-start = ((), (), s32[]{:S(2)}) async-start(), calls=%async_computation.7 | async-start | bytes 3899392 | tf_op jit(solution)/shard_map/all_gather | solution.py:112
  19.1 16.3 %all-to-all-start.1 = ((bf16[128,16,128]{2,0,1:T(8,128)(2,1)}), bf16[128,16,128]{2,0,1:T(8,128)(2,1)S(1)}, u32[]{:S(2)}, u32[]{:S(2)}) async-start(bf16[128,16,128]{2,0,1:T(8,128)(2,1)} %copy_bitcast_fusion.2), calls=%async_computation.1 | async-start | bytes 1048576 | tf_op jit(solution)/shard_map/all_to_all | solution.py:86
  24.5 71.5 %copy-start.4 = (s32[128,8]{0,1:T(8,128)S(1)}, s32[128,8]{0,1:T(8,128)}, u32[]{:S(2)}) copy-start(s32[128,8]{0,1:T(8,128)} %param.26) | copy-start | bytes 12292
  35.3 14.4 %all-to-all-start.2 = ((bf16[128,16,128]{2,0,1:T(8,128)(2,1)}), bf16[128,16,128]{2,0,1:T(8,128)(2,1)S(1)}, u32[]{:S(2)}, u32[]{:S(2)}) async-start(bf16[128,16,128]{2,0,1:T(8,128)(2,1)} %copy_bitcast_fusion.1), calls=%async_computation.2 | async-start | bytes 1048576 | tf_op jit(solution)/shard_map/all_to_all | solution.py:87
  49.7 16.8 %all-to-all-start = ((bf16[128,16,128]{2,0,1:T(8,128)(2,1)}), bf16[128,16,128]{2,0,1:T(8,128)(2,1)S(1)}, u32[]{:S(2)}, u32[]{:S(2)}) async-start(bf16[128,16,128]{2,0,1:T(8,128)(2,1)} %copy_bitcast_fusion.3), calls=%async_computation | async-start | bytes 1048576 | tf_op jit(solution)/shard_map/all_to_all | solution.py:85
  53.3 117.8 %all-gather.4.cloned.1.call-start = ((), (), s32[]{:S(2)}) async-start(), calls=%async_computation.6 | async-start | bytes 8912896 | tf_op jit(solution)/shard_map/all_gather | solution.py:118
  108.5 18.8 %all-to-all-start.3 = ((bf16[16,128,128]{2,1,0:T(8,128)(2,1)}), bf16[16,128,128]{2,1,0:T(8,128)(2,1)S(1)}, u32[]{:S(2)}, u32[]{:S(2)}) async-start(bf16[16,128,128]{2,1,0:T(8,128)(2,1)} %bitcast.35), calls=%async_computation.3 | async-start | bytes 1048576 | tf_op jit(solution)/shard_map/all_to_all | solution.py:129
  116.6 54.5 %copy-start.1 = (bf16[128,2048]{1,0:T(8,128)(2,1)S(1)}, bf16[128,2048]{1,0:T(8,128)(2,1)}, u32[]{:S(2)}) copy-start(bf16[128,2048]{1,0:T(8,128)(2,1)} %param.15) | copy-start | bytes 1572868
  171.1 6.4 %copy-start.7 = (f32[2048]{0:T(1024)S(1)}, f32[2048]{0:T(1024)}, u32[]{:S(2)}) copy-start(f32[2048]{0:T(1024)} %param.22) | copy-start | bytes 24580
  177.4 10.7 %copy-start.2 = (bf16[128,2048]{1,0:T(8,128)(2,1)}, bf16[128,2048]{1,0:T(8,128)(2,1)S(1)}, u32[]{:S(2)}) copy-start(bf16[128,2048]{1,0:T(8,128)(2,1)S(1)} %get-tuple-element.106) | copy-start | bytes 1572868
  179.0 22.6 %all-to-all-start.4 = ((bf16[16,16,2048]{2,1,0:T(8,128)(2,1)}), bf16[16,16,2048]{2,1,0:T(8,128)(2,1)}, u32[]{:S(2)}, u32[]{:S(2)}) async-start(bf16[16,16,2048]{2,1,0:T(8,128)(2,1)} %bitcast.41), calls=%async_computation.4 | async-start | bytes 2097152 | tf_op jit(solution)/shard_map/all_to_all | solution.py:151
  195.4 16.0 %copy-start.5 = (f32[128,8]{0,1:T(8,128)S(1)}, f32[128,8]{0,1:T(8,128)}, u32[]{:S(2)}) copy-start(f32[128,8]{0,1:T(8,128)} %param.27) | copy-start | bytes 12292
  207.7 20.1 %all-to-all-start.5 = ((bf16[16,16,2048]{2,1,0:T(8,128)(2,1)}), bf16[16,16,2048]{2,1,0:T(8,128)(2,1)S(1)}, u32[]{:S(2)}, u32[]{:S(2)}) async-start(bf16[16,16,2048]{2,1,0:T(8,128)(2,1)} %convolution_convert_fusion), calls=%async_computation.5 | async-start | bytes 2097152 | tf_op jit(solution)/shard_map/all_to_all | solution.py:158
Sparse Core Ops, SparseCore 0:
  18.2 75.7 all-gather.5
  96.7 74.3 all-gather.3
where the time goes:
time: 238 us; the launch traced here: 237 us
  waiting for transfers between devices  117 us (49%)
  local copies, waits for them, and re-layouts  37.5 us (16%)
  starting transfers between devices  27.6 us (12%)
  matrix products  24 us (10%)
  between operations  14.3 us (6%)
  other arithmetic  8.66 us (4%)
  blocking collectives  7.16 us (3%)
    all_gather x1, waiting for transfers between devices, body(): wo_full = lax.all_gather(wo_cols, 'tensor', axis=1, tiled=True)  43.4 us
    all_gather x1, waiting for transfers between devices, body(): gathered = lax.all_gather(lax.all_gather(packed, 'dh'), 'dz')  27.6 us
    all_to_all x1, waiting for transfers between devices, body(): lax.all_to_all(result, 'tensor', split_axis=0, concat_axis=0, tiled=True)  16.4 us
    all_to_all x1, waiting for transfers between devices, body(): lax.all_to_all(new_values, 'tensor', split_axis=1, concat_axis=0, tiled=T...  9.71 us
    all_gather x1, blocking collectives, body(): gathered = lax.all_gather(lax.all_gather(packed, 'dh'), 'dz')  7.16 us
    all_to_all x1, waiting for transfers between devices, body(): lax.all_to_all(attended, 'tensor', split_axis=0, concat_axis=1, tiled=True)  7 us
    all_to_all x1, waiting for transfers between devices, body(): lax.all_to_all(new_keys, 'tensor', split_axis=1, concat_axis=0, tiled=True)  6.95 us
    scatter x1, local copies, waits for them, and re-layouts, body(): value_pages = jnp.zeros((pool_size * PAGE, head_width), jnp.bfloat16).at[...  6.54 us
  transfers between devices with their start and end apart: 8, of which 7 were waited for; matrix products, arithmetic and copies ran while one was open for 21% of the time, Pallas kernels for 0%

commit v1 on v0

--- a/solution.py
+++ b/solution.py
@@ -115,7 +115,9 @@
     )
     wo_piece_rows = pieces[0].size // 128
     wo_cols = jnp.swapaxes(gathered[:, :, :wo_piece_rows], 0, 1).reshape(-1, pieces[0].shape[1])
-    wo_full = lax.all_gather(wo_cols, "tensor", axis=1, tiled=True)
+    wo_full = jnp.concatenate(
+        lax.all_to_all(jnp.stack([wo_cols] * lax.axis_size("tensor")), "tensor", 0, 0), axis=1
+    )
     experts = jnp.swapaxes(gathered[:, :, wo_piece_rows:], 0, 1)
     experts = experts.reshape(experts.shape[0] * experts.shape[1], -1)
     weights_full, at = ([], 0)

time: 238 us -> 338 us (1.42)
  the two profiles are of different devices: /device:TPU:224 before, /device:TPU:1 now
where the time goes in v1:
time: 338 us; the launch traced here: 336 us
  waiting for transfers between devices  186 us (55%)
  starting transfers between devices  55.3 us (16%)
  local copies, waits for them, and re-layouts  41.9 us (12%)
  matrix products  23.9 us (7%)
  between operations  14.2 us (4%)
  other arithmetic  8.65 us (3%)
  blocking collectives  6.67 us (2%)
    all_to_all x1, waiting for transfers between devices, body(): lax.all_to_all(jnp.stack([wo_cols] * lax.axis_size('tensor')), 'tensor',...  121 us
    all_gather x1, waiting for transfers between devices, body(): gathered = lax.all_gather(lax.all_gather(packed, 'dh'), 'dz')  20.5 us
    all_to_all x1, waiting for transfers between devices, body(): lax.all_to_all(result, 'tensor', split_axis=0, concat_axis=0, tiled=True)  15.5 us
    all_to_all x1, starting transfers between devices, body(): lax.all_to_all(attended, 'tensor', split_axis=0, concat_axis=1, tiled=True)  14.8 us
    all_to_all x1, starting transfers between devices, body(): lax.all_to_all(new_keys, 'tensor', split_axis=1, concat_axis=0, tiled=True)  10.6 us
    all_to_all x1, starting transfers between devices, body(): lax.all_to_all(outgoing, 'tensor', split_axis=0, concat_axis=0, tiled=True)  10.2 us
    all_to_all x1, waiting for transfers between devices, body(): lax.all_to_all(new_values, 'tensor', split_axis=1, concat_axis=0, tiled=T...  8.68 us
    all_to_all x1, waiting for transfers between devices, body(): lax.all_to_all(attended, 'tensor', split_axis=0, concat_axis=1, tiled=True)  8.57 us
  transfers between devices with their start and end apart: 8, of which 7 were waited for; matrix products, arithmetic and copies ran while one was open for 11% of the time, Pallas kernels for 0%

profile of v1, /device:TPU:1, one launch (start us, length us, event | category | flops | bytes accessed | tf_op | source)
XLA Modules:
  0.0 336.5 jit_solution(10735120357280760331)
XLA Ops:
  7.2 0.8 convert_bitcast_fusion.2
  8.1 0.8 convert_bitcast_fusion.1
  9.0 0.8 convert_bitcast_fusion
  9.8 0.8 convert_element_type.85
  10.7 0.1 copy.62
  10.8 0.1 convert_element_type.86
  10.9 6.7 %all_gather.9 = bf16[2,448,128]{2,1,0:T(8,128)(2,1)} all-gather(bf16[1,448,128]{2,1,0:T(8,128)(2,1)S(1)} %maximum_bitcast_fusion), channel_id=1, replica_groups=mesh['dh'=2,'dz'=16,'tensor'=16] {'dh'}, dimensions={0}, use_global_device_ids=true | all-gather | bytes 344064 | tf_op jit(solution)/shard_map/all_gather | solution.py:112
  17.6 0.9 copy_bitcast_fusion.2
  18.6 10.6 %all-to-all-start.1 = ((bf16[128,16,128]{2,0,1:T(8,128)(2,1)}), bf16[128,16,128]{2,0,1:T(8,128)(2,1)S(1)}, u32[]{:S(2)}, u32[]{:S(2)}) async-start(bf16[128,16,128]{2,0,1:T(8,128)(2,1)} %copy_bitcast_fusion.2), calls=%async_computation.1 | async-start | bytes 1048576 | tf_op jit(solution)/shard_map/all_to_all | solution.py:86
  29.2 0.8 reduce-window.6
  30.0 0.7 and_select_fusion.1
  30.7 0.2 reduce-window_1_clone.1
  30.9 0.1 select_reduce_fusion.2
  31.0 2.0 copy_bitcast_fusion.1
  33.0 5.9 %all-to-all-done.1 = bf16[128,16,128]{2,0,1:T(8,128)(2,1)S(1)} async-done(((bf16[128,16,128]{2,0,1:T(8,128)(2,1)}), bf16[128,16,128]{2,0,1:T(8,128)(2,1)S(1)}, u32[]{:S(2)}, u32[]{:S(2)}) %all-to-all-start.1) | async-done | bytes 524320 | tf_op jit(solution)/shard_map/all_to_all | solution.py:86
  38.9 4.6 %all-to-all-start.2 = ((bf16[128,16,128]{2,0,1:T(8,128)(2,1)}), bf16[128,16,128]{2,0,1:T(8,128)(2,1)S(1)}, u32[]{:S(2)}, u32[]{:S(2)}) async-start(bf16[128,16,128]{2,0,1:T(8,128)(2,1)} %copy_bitcast_fusion.1), calls=%async_computation.2 | async-start | bytes 1048576 | tf_op jit(solution)/shard_map/all_to_all | solution.py:87
  43.6 0.1 select_reduce_fusion
  43.7 0.9 copy_bitcast_fusion.3
  44.6 8.7 %all-to-all-done.2 = bf16[128,16,128]{2,0,1:T(8,128)(2,1)S(1)} async-done(((bf16[128,16,128]{2,0,1:T(8,128)(2,1)}), bf16[128,16,128]{2,0,1:T(8,128)(2,1)S(1)}, u32[]{:S(2)}, u32[]{:S(2)}) %all-to-all-start.2) | async-done | bytes 524320 | tf_op jit(solution)/shard_map/all_to_all | solution.py:87
  53.3 4.6 %all-to-all-start = ((bf16[128,16,128]{2,0,1:T(8,128)(2,1)}), bf16[128,16,128]{2,0,1:T(8,128)(2,1)S(1)}, u32[]{:S(2)}, u32[]{:S(2)}) async-start(bf16[128,16,128]{2,0,1:T(8,128)(2,1)} %copy_bitcast_fusion.3), calls=%async_computation | async-start | bytes 1048576 | tf_op jit(solution)/shard_map/all_to_all | solution.py:85
  58.0 6.5 %scatter_custom_fusion.1 = bf16[2176,128]{1,0:T(8,128)(2,1)} fusion(s32[2048]{0:T(1024)S(1)} %bitcast.177, bf16[2048,128]{1,0:T(8,128)(2,1)S(1)} %bitcast.158, bf16[]{:T(256)} %constant.81.clone.1), kind=kCustom, calls=%fused_computation.46 | custom fusion | bytes 557058 | tf_op jit(solution)/shard_map/scatter | solution.py:102
  64.5 6.5 %scatter_custom_fusion = bf16[2176,128]{1,0:T(8,128)(2,1)} fusion(s32[2048]{0:T(1024)S(1)} %bitcast.178, bf16[2048,128]{1,0:T(8,128)(2,1)S(1)} %bitcast.169, bf16[]{:T(256)} %constant.81.clone.1), kind=kCustom, calls=%fused_computation.48 | custom fusion | bytes 557058 | tf_op jit(solution)/shard_map/scatter | solution.py:96
  71.1 20.5 %all-gather.3.cloned.1.call-done = bf16[32,448,128]{2,1,0:T(8,128)(2,1)} async-done(((bf16[2,448,128]{2,1,0:T(8,128)(2,1)}), bf16[32,448,128]{2,1,0:T(8,128)(2,1)}) %all-gather.3.cloned.1.call-update) | async-done | bytes 3670032 | tf_op jit(solution)/shard_map/all_gather | solution.py:112
  91.6 12.2 %while.10 = (s32[]{:T(128)}, bf16[4,512,128]{2,1,0:T(8,128)(2,1)}, s32[4,512]{1,0:T(4,128)S(1)}, s32[2048]{0:T(1024)S(1)}, bf16[4,512,1,128]{3,1,2,0:T(8,128)(2,...) while((s32[]{:T(128)}, bf16[4,512,128]{2,1,0:T(8,128)(2,1)}, ...), condition=%wide.region_11.12_spmd, body=%wide.region_8.11_spmd.sunk | while | flops 545389568 | bytes 13918313 | solution.py:64
  91.6 0.9 fusion.95
  92.5 0.7 fusion.96
  93.2 1.5 fusion.97
  94.6 0.9 fusion.95
  95.5 0.7 fusion.96
  96.2 1.5 fusion.97
  97.7 0.9 fusion.95
  98.6 0.7 fusion.96
  99.3 1.5 fusion.97
  100.7 0.9 fusion.95
  101.6 0.7 fusion.96
  102.3 1.5 fusion.97
  103.8 14.8 %all-to-all-start.3 = ((bf16[16,128,128]{2,1,0:T(8,128)(2,1)}), bf16[16,128,128]{2,1,0:T(8,128)(2,1)S(1)}, u32[]{:S(2)}, u32[]{:S(2)}) async-start(bf16[16,128,128]{2,1,0:T(8,128)(2,1)} %bitcast.35), calls=%async_computation.3 | async-start | bytes 1048576 | tf_op jit(solution)/shard_map/all_to_all | solution.py:131
  118.6 1.1 slice_bitcast_fusion.1
  119.7 8.6 %all-to-all-done.3 = bf16[16,128,128]{2,1,0:T(8,128)(2,1)S(1)} async-done(((bf16[16,128,128]{2,1,0:T(8,128)(2,1)}), bf16[16,128,128]{2,1,0:T(8,128)(2,1)S(1)}, u32[]{:S(2)}, u32[]{:S(2)}) %all-to-all-start.3) | async-done | bytes 524320 | tf_op jit(solution)/shard_map/all_to_all | solution.py:131
  128.3 4.8 %stack.3 = bf16[16,2048,128]{2,1,0:T(8,128)(2,1)} broadcast(bf16[2048,128]{1,0:T(8,128)(2,1)S(1)} %bitcast.165), dimensions={1,2} | broadcast | bytes 8912896 | tf_op jit(solution)/shard_map/stack | solution.py:119
  133.1 5.8 %all-to-all-start.4 = ((bf16[16,2048,128]{2,1,0:T(8,128)(2,1)}), bf16[16,2048,128]{2,1,0:T(8,128)(2,1)}, u32[]{:S(2)}, u32[]{:S(2)}) async-start(bf16[16,2048,128]{2,1,0:T(8,128)(2,1)} %stack.3), calls=%async_computation.4 | async-start | bytes 16777216 | tf_op jit(solution)/shard_map/all_to_all | solution.py:119
  139.0 0.1 copy.68
  139.1 0.2 reduce_window_sum.20
  139.3 2.2 slice_bitcast_fusion
  141.6 0.3 copy.70
  141.9 3.7 %copy.85 = bf16[4,8,384,128]{3,1,2,0:T(8,128)(2,1)} copy(bf16[4,8,384,128]{3,2,1,0:T(8,128)(2,1)S(1)} %bitcast.161) | data formatting | bytes 6291456
  145.6 121.4 %all-to-all-done.4 = bf16[16,2048,128]{2,1,0:T(8,128)(2,1)} async-done(((bf16[16,2048,128]{2,1,0:T(8,128)(2,1)}), bf16[16,2048,128]{2,1,0:T(8,128)(2,1)}, u32[]{:S(2)}, u32[]{:S(2)}) %all-to-all-start.4) | async-done | bytes 8388640 | tf_op jit(solution)/shard_map/all_to_all | solution.py:119
  267.0 6.3 %fusion.38 = (f32[128]{0:T(128)S(1)}, bf16[128,2048]{1,0:T(8,128)(2,1)S(1)}) fusion(bf16[16,2048,128]{2,1,0:T(8,128)(2,1)} %all-to-all-done.4, bf16[16,128,128]{2,1,0:T(8,128)(2,1)S(1)} %all-to-all-done.3, bf16[128,2048]{1,0:T(8,128)(2,1)S(1)} %copy-done.1), kind=kOutput, calls=%fused_computation.35 | convolution fusion | flops 1075314560 | bytes 9961984 | tf_op jit(solution)/shard_map/tr,cr->tc/dot_general | solution.py:132
  273.3 0.8 copy-done.2
  274.1 0.3 convolution_convert_fusion.1
  274.4 1.2 broadcast_in_dim.27
  275.6 10.2 %all-to-all-start.5 = ((bf16[16,16,2048]{2,1,0:T(8,128)(2,1)}), bf16[16,16,2048]{2,1,0:T(8,128)(2,1)}, u32[]{:S(2)}, u32[]{:S(2)}) async-start(bf16[16,16,2048]{2,1,0:T(8,128)(2,1)} %bitcast.42), calls=%async_computation.5 | async-start | bytes 2097152 | tf_op jit(solution)/shard_map/all_to_all | solution.py:153
  285.8 3.0 fusion.77
  288.8 1.3 reshape.280
  290.2 1.3 reshape.281
  291.5 3.0 reshape.259
  294.5 1.6 copy.71
  296.1 5.2 %all-to-all-done.5 = bf16[16,16,2048]{2,1,0:T(8,128)(2,1)} async-done(((bf16[16,16,2048]{2,1,0:T(8,128)(2,1)}), bf16[16,16,2048]{2,1,0:T(8,128)(2,1)}, u32[]{:S(2)}, u32[]{:S(2)}) %all-to-all-start.5) | async-done | bytes 1048608 | tf_op jit(solution)/shard_map/all_to_all | solution.py:153
  301.3 2.0 fusion.78
  303.3 4.2 %convolution_convert_fusion = bf16[16,16,2048]{2,1,0:T(8,128)(2,1)} fusion(bf16[256,2048,1]{0,1,2:T(8,128)(2,1)} %bitcast.166, bf16[16,16,2048]{2,1,0:T(8,128)(2,1)} %all-to-all-done.5, bf16[2048,256,1]{1,0,2:T(8,128)(2,1)} %reshape.281, f32[16,16,256]{2,1,0:T(8,128)S(1)} %fusion.78), kind=kOutput, calls=%fused_computation.23 | convolution fusion | flops 537788416 | bytes 4456448 | tf_op jit(solution)/shard_map/smp,pd->smd/dot_general | solution.py:157
  307.5 4.5 %all-to-all-start.6 = ((bf16[16,16,2048]{2,1,0:T(8,128)(2,1)}), bf16[16,16,2048]{2,1,0:T(8,128)(2,1)S(1)}, u32[]{:S(2)}, u32[]{:S(2)}) async-start(bf16[16,16,2048]{2,1,0:T(8,128)(2,1)} %convolution_convert_fusion), calls=%async_computation.6 | async-start | bytes 2097152 | tf_op jit(solution)/shard_map/all_to_all | solution.py:160
  312.1 15.5 %all-to-all-done.6 = bf16[16,16,2048]{2,1,0:T(8,128)(2,1)S(1)} async-done(((bf16[16,16,2048]{2,1,0:T(8,128)(2,1)}), bf16[16,16,2048]{2,1,0:T(8,128)(2,1)S(1)}, u32[]{:S(2)}, u32[]{:S(2)}) %all-to-all-start.6) | async-done | bytes 1048608 | tf_op jit(solution)/shard_map/all_to_all | solution.py:160
  327.6 0.2 convert_reduce_fusion
  327.8 1.8 fusion.36
  (39 shorter events, 0.5 us)
Async XLA Ops:
  7.2 10.5 %copy-start = (bf16[128,2048]{1,0:T(8,128)(2,1)S(1)}, bf16[128,2048]{1,0:T(8,128)(2,1)}, u32[]{:S(2)}) copy-start(bf16[128,2048]{1,0:T(8,128)(2,1)} %param.17) | copy-start | bytes 1572868
  7.2 36.4 %copy-start.6 = (s32[1,17]{1,0:T(1,128)S(1)}, s32[1,17]{1,0:T(1,128)}, u32[]{:S(2)}) copy-start(s32[1,17]{1,0:T(1,128)} %param.20) | copy-start | bytes 208
  7.2 36.5 %copy-start.3 = (bf16[128,2048]{1,0:T(8,128)(2,1)S(1)}, bf16[128,2048]{1,0:T(8,128)(2,1)}, u32[]{:S(2)}) copy-start(bf16[128,2048]{1,0:T(8,128)(2,1)} %param.16) | copy-start | bytes 1572868
  7.2 84.4 %all-gather.3.cloned.1.call-start = ((), (), s32[]{:S(2)}) async-start(), calls=%async_computation.7 | async-start | bytes 3899392 | tf_op jit(solution)/shard_map/all_gather | solution.py:112
  18.6 20.4 %all-to-all-start.1 = ((bf16[128,16,128]{2,0,1:T(8,128)(2,1)}), bf16[128,16,128]{2,0,1:T(8,128)(2,1)S(1)}, u32[]{:S(2)}, u32[]{:S(2)}) async-start(bf16[128,16,128]{2,0,1:T(8,128)(2,1)} %copy_bitcast_fusion.2), calls=%async_computation.1 | async-start | bytes 1048576 | tf_op jit(solution)/shard_map/all_to_all | solution.py:86
  38.9 14.4 %all-to-all-start.2 = ((bf16[128,16,128]{2,0,1:T(8,128)(2,1)}), bf16[128,16,128]{2,0,1:T(8,128)(2,1)S(1)}, u32[]{:S(2)}, u32[]{:S(2)}) async-start(bf16[128,16,128]{2,0,1:T(8,128)(2,1)} %copy_bitcast_fusion.1), calls=%async_computation.2 | async-start | bytes 1048576 | tf_op jit(solution)/shard_map/all_to_all | solution.py:87
  53.3 17.8 %all-to-all-start = ((bf16[128,16,128]{2,0,1:T(8,128)(2,1)}), bf16[128,16,128]{2,0,1:T(8,128)(2,1)S(1)}, u32[]{:S(2)}, u32[]{:S(2)}) async-start(bf16[128,16,128]{2,0,1:T(8,128)(2,1)} %copy_bitcast_fusion.3), calls=%async_computation | async-start | bytes 1048576 | tf_op jit(solution)/shard_map/all_to_all | solution.py:85
  103.8 24.5 %all-to-all-start.3 = ((bf16[16,128,128]{2,1,0:T(8,128)(2,1)}), bf16[16,128,128]{2,1,0:T(8,128)(2,1)S(1)}, u32[]{:S(2)}, u32[]{:S(2)}) async-start(bf16[16,128,128]{2,1,0:T(8,128)(2,1)} %bitcast.35), calls=%async_computation.3 | async-start | bytes 1048576 | tf_op jit(solution)/shard_map/all_to_all | solution.py:131
  133.1 5.8 %copy-start.4 = (s32[128,8]{0,1:T(8,128)S(1)}, s32[128,8]{0,1:T(8,128)}, u32[]{:S(2)}) copy-start(s32[128,8]{0,1:T(8,128)} %param.26) | copy-start | bytes 12292
  133.1 133.9 %all-to-all-start.4 = ((bf16[16,2048,128]{2,1,0:T(8,128)(2,1)}), bf16[16,2048,128]{2,1,0:T(8,128)(2,1)}, u32[]{:S(2)}, u32[]{:S(2)}) async-start(bf16[16,2048,128]{2,1,0:T(8,128)(2,1)} %stack.3), calls=%async_computation.4 | async-start | bytes 16777216 | tf_op jit(solution)/shard_map/all_to_all | solution.py:119
  141.9 125.1 %copy-start.1 = (bf16[128,2048]{1,0:T(8,128)(2,1)S(1)}, bf16[128,2048]{1,0:T(8,128)(2,1)}, u32[]{:S(2)}) copy-start(bf16[128,2048]{1,0:T(8,128)(2,1)} %param.15) | copy-start | bytes 1572868
  145.6 128.5 %copy-start.7 = (f32[2048]{0:T(1024)S(1)}, f32[2048]{0:T(1024)}, u32[]{:S(2)}) copy-start(f32[2048]{0:T(1024)} %param.22) | copy-start | bytes 24580
  273.3 0.8 copy-start.2
  275.6 25.8 %all-to-all-start.5 = ((bf16[16,16,2048]{2,1,0:T(8,128)(2,1)}), bf16[16,16,2048]{2,1,0:T(8,128)(2,1)}, u32[]{:S(2)}, u32[]{:S(2)}) async-start(bf16[16,16,2048]{2,1,0:T(8,128)(2,1)} %bitcast.42), calls=%async_computation.5 | async-start | bytes 2097152 | tf_op jit(solution)/shard_map/all_to_all | solution.py:153
  296.1 15.9 %copy-start.5 = (f32[128,8]{0,1:T(8,128)S(1)}, f32[128,8]{0,1:T(8,128)}, u32[]{:S(2)}) copy-start(f32[128,8]{0,1:T(8,128)} %param.27) | copy-start | bytes 12292
  307.5 20.1 %all-to-all-start.6 = ((bf16[16,16,2048]{2,1,0:T(8,128)(2,1)}), bf16[16,16,2048]{2,1,0:T(8,128)(2,1)S(1)}, u32[]{:S(2)}, u32[]{:S(2)}) async-start(bf16[16,16,2048]{2,1,0:T(8,128)(2,1)} %convolution_convert_fusion), calls=%async_computation.6 | async-start | bytes 2097152 | tf_op jit(solution)/shard_map/all_to_all | solution.py:160
Sparse Core Ops, SparseCore 0:
  17.7 73.7 all-gather.2
